TPU v7x, 256 devices: a whole 4x4x8 slice. The times are simulated.
256 devices in a mesh: row: 32 (over z, y), col: 8 (over x, core).
Axes of the slice: x: 4, y: 4, z: 8, core: 2. Of those that a mesh axis runs over, the one named last changes fastest.
Arguments:
- saved_input: bfloat16 [1024, 49152], P('col', 'row'), may hold values from -6 to 6
- out_grad: bfloat16 [1024, 12288], P('row', 'col'), may hold values from -0.75 to 0.75
- weight: bfloat16 [49152, 12288], P('row', 'col'), may hold values from -0.625 to 0.625
Outputs:
- in_grad: bfloat16 [1024, 49152], P('col', 'row')
- weight_grad: bfloat16 [49152, 12288], P('row', 'col')
All inputs are finite; a program needn't handle non-finite values.
Results may differ from a plain program's by a relative error of at most 0.0051.
Values may be sent and summed in bfloat16 or wider, within the bound.
No kernel may reach another device: no remote copies, remote signals or barrier semaphores. Data moves between devices by JAX's collectives and lax.ppermute only.
A program may use at most 64 MiB of HBM per device.

v0:
```python
import math
import jax
import jax.numpy as jnp
from jax import lax
from jax.sharding import PartitionSpec as P


def gelu_parts(values):
    coeff = math.sqrt(2.0 / math.pi)
    inner = jnp.tanh(coeff * (values + 0.044715 * values * values * values))
    gelu_value = 0.5 * values * (1.0 + inner)
    gelu_slope = 0.5 * (1.0 + inner) + 0.5 * values * (1.0 - inner * inner) * coeff * (
        1.0 + 3.0 * 0.044715 * values * values
    )
    return (gelu_value, gelu_slope)


def per_device(saved_input, out_grad, weight):
    grad_all = lax.all_gather(out_grad, "row", axis=0, tiled=True)
    saved_all = lax.all_gather(saved_input, "col", axis=0, tiled=True)
    gelu_value, unused_slope = gelu_parts(saved_all.astype(jnp.float32))
    hidden = gelu_value.astype(jnp.bfloat16)
    weight_grad = lax.dot_general(
        hidden, grad_all, (((0,), (0,)), ((), ())), preferred_element_type=jnp.float32
    ).astype(jnp.bfloat16)
    back = lax.psum_scatter(
        lax.dot_general(
            grad_all, weight, (((1,), (1,)), ((), ())), preferred_element_type=jnp.float32
        ),
        "col",
        scatter_dimension=0,
        tiled=True,
    )
    unused_value, own_slope = gelu_parts(saved_input.astype(jnp.float32))
    in_grad = (back * own_slope).astype(jnp.bfloat16)
    return (in_grad, weight_grad)


def solution(mesh):
    in_specs = (P("col", "row"), P("row", "col"), P("row", "col"))
    out_specs = (P("col", "row"), P("row", "col"))
    return jax.shard_map(
        per_device, mesh=mesh, in_specs=in_specs, out_specs=out_specs, check_vma=False
    )
```

profile of v0, /device:TPU:1, one launch (start us, length us, event | category | flops | bytes accessed | tf_op | source)
XLA Modules:
  0.0 178.5 jit_solution(13680003618552402031)
XLA Ops:
  7.2 0.0 all-gather.3.cloned.1.call-start
  7.2 0.7 all-gather.3.cloned.1.call-update
  7.9 0.0 all-gather.5.cloned.1.call-start
  7.9 0.7 all-gather.5.cloned.1.call-update
  8.6 0.0 reduce-scatter.2.cloned.1.call-start
  8.7 81.3 %all-gather.3.cloned.1.call-done = bf16[1024,1536]{1,0:T(8,128)(2,1)} async-done(((bf16[32,1536]{1,0:T(8,128)(2,1)}), bf16[1024,1536]{1,0:T(8,128)(2,1)}) %all-gather.3.cloned.1.call-update) | async-done | bytes 3145744 | tf_op jit(solution)/shard_map/all_gather | solution.py:19
  90.0 9.8 %fusion.23 = f32[1024,1536]{1,0:T(8,128)} fusion(bf16[1024,1536]{1,0:T(8,128)(2,1)} %all-gather.3.cloned.1.call-done, bf16[1536,1536]{1,0:T(8,128)(2,1)} %param.5), kind=kOutput, calls=%fused_computation.35 | convolution fusion | flops 4831838208 | bytes 14155776 | tf_op jit(solution)/shard_map/dot_general | solution.py:27
  99.7 0.0 copy-start.1
  99.7 0.0 reduce-scatter.2.cloned.1.call-update
  99.8 0.0 copy-start
  99.8 23.2 %all-gather.5.cloned.1.call-done = bf16[1024,1536]{1,0:T(8,128)(2,1)} async-done(((bf16[128,1536]{1,0:T(8,128)(2,1)}), bf16[1024,1536]{1,0:T(8,128)(2,1)}) %all-gather.5.cloned.1.call-update) | async-done | bytes 3145744 | tf_op jit(solution)/shard_map/all_gather | solution.py:20
  122.9 0.0 copy-done.1
  122.9 11.2 %convolution_convert_fusion = bf16[1536,1536]{1,0:T(8,128)(2,1)} fusion(bf16[1024,1536]{1,0:T(8,128)(2,1)S(1)} %copy-done.1, bf16[1024,1536]{1,0:T(8,128)(2,1)} %all-gather.5.cloned.1.call-done), kind=kOutput, calls=%fused_computation.5 | convolution fusion | flops 4849926144 | bytes 11010048 | tf_op jit(solution)/shard_map/dot_general | solution.py:23
  134.2 35.4 %reduce-scatter.2.cloned.1.call-done = f32[128,1536]{1,0:T(8,128)} async-done(((f32[1024,1536]{1,0:T(8,128)}), f32[128,1536]{1,0:T(8,128)}) %reduce-scatter.2.cloned.1.call-update) | async-done | bytes 786448 | tf_op jit(solution)/shard_map/reduce_scatter | solution.py:26
  169.6 0.0 copy-done
  169.6 2.4 %fusion.17 = bf16[128,1536]{1,0:T(8,128)(2,1)} fusion(f32[128,1536]{1,0:T(8,128)} %reduce-scatter.2.cloned.1.call-done, bf16[128,1536]{1,0:T(8,128)(2,1)S(1)} %copy-done), kind=kLoop, calls=%fused_computation.29 | loop fusion | flops 3932160 | bytes 1572864 | tf_op jit(solution)/shard_map/convert_element_type | solution.py:35
Async XLA Ops:
  7.2 82.8 %all-gather.3.cloned.1.call-start = ((), (), s32[]{:S(2)}) async-start(), calls=%async_computation.1 | async-start | bytes 3244032 | tf_op jit(solution)/shard_map/all_gather | solution.py:19
  7.9 115.0 %all-gather.5.cloned.1.call-start = ((), (), s32[]{:S(2)}) async-start(), calls=%async_computation.3 | async-start | bytes 3538944 | tf_op jit(solution)/shard_map/all_gather | solution.py:20
  8.6 161.0 %reduce-scatter.2.cloned.1.call-start = ((), (), s32[]{:S(2)}) async-start(), calls=%async_computation.2 | async-start | bytes 7077888 | tf_op jit(solution)/shard_map/reduce_scatter | solution.py:26
  99.7 23.2 %copy-start.1 = (bf16[1024,1536]{1,0:T(8,128)(2,1)S(1)}, bf16[1024,1536]{1,0:T(8,128)(2,1)}, u32[]{:S(2)}) copy-start(bf16[1024,1536]{1,0:T(8,128)(2,1)} %all-gather.3.cloned.1.call-done) | copy-start | bytes 9437188
  99.8 69.8 %copy-start = (bf16[128,1536]{1,0:T(8,128)(2,1)S(1)}, bf16[128,1536]{1,0:T(8,128)(2,1)}, u32[]{:S(2)}) copy-start(bf16[128,1536]{1,0:T(8,128)(2,1)} %param.3) | copy-start | bytes 1179652
Sparse Core Ops, SparseCore 0:
  10.5 79.3 all-gather.2
  91.8 31.1 all-gather.4
  125.5 44.0 reduce-scatter.1
where the time goes:
time: 179 us
  waiting for transfers between devices  141 us (79%)
  matrix products  21 us (12%)
  between operations  13.8 us (8%)
  other arithmetic  2.4 us (1%)
    all_gather x1, waiting for transfers between devices, per_device(): grad_all = lax.all_gather(out_grad, 'row', axis=0, tiled=True)  81.3 us
    reduce_scatter x1, waiting for transfers between devices, per_device(): lax.psum_scatter(lax.dot_general(grad_all, weight, (((1,), (1,)), ((), ()...  35.4 us
    all_gather x1, waiting for transfers between devices, per_device(): saved_all = lax.all_gather(saved_input, 'col', axis=0, tiled=True)  23.2 us
    dot_general x1, matrix products, per_device(): lax.dot_general(hidden, grad_all, (((0,), (0,)), ((), ())), preferred_ele...  11.2 us
    dot_general x1, matrix products, per_device(): lax.dot_general(grad_all, weight, (((1,), (1,)), ((), ())), preferred_ele...  9.78 us
  transfers between devices with their start and end apart: 3, of which 3 were waited for; matrix products, arithmetic and copies ran while one was open for 12% of the time, Pallas kernels for 0%

commit v1 on v0

--- a/solution.py
+++ b/solution.py
@@ -17,7 +17,9 @@
 
 def per_device(saved_input, out_grad, weight):
     grad_all = lax.all_gather(out_grad, "row", axis=0, tiled=True)
-    saved_all = lax.all_gather(saved_input, "col", axis=0, tiled=True)
+    saved_all = jnp.concatenate(
+        lax.all_to_all(jnp.stack([saved_input] * lax.axis_size("col")), "col", 0, 0), axis=0
+    )
     gelu_value, unused_slope = gelu_parts(saved_all.astype(jnp.float32))
     hidden = gelu_value.astype(jnp.bfloat16)
     weight_grad = lax.dot_general(

time: 179 us -> 186 us (1.039)
  blocking collectives: 0 us -> 62.3 us
  waiting for transfers between devices: 141 us -> 89.1 us
  matrix products: 21 us -> 17.1 us
    all_to_all x0 -> x1, blocking collectives: none -> 62.3 us  [per_device(): lax.all_to_all(jnp.stack([saved_input] * lax.axis_size('col')), 'col', 0, 0)]
    reduce_scatter x1, waiting for transfers between devices: 35.4 us -> 6.37 us  [per_device(): lax.psum_scatter(lax.dot_general(grad_all, weight, (((1,), (1,)), ((), ()...]
    all_gather x1 -> x0, waiting for transfers between devices: 23.2 us -> none  [per_device(): saved_all = lax.all_gather(saved_input, 'col', axis=0, tiled=True)]
    dot_general x1, matrix products: 11.2 us -> 7.33 us  [per_device(): lax.dot_general(hidden, grad_all, (((0,), (0,)), ((), ())), preferred_ele...]
  transfers between devices with their start and end apart: 3 -> 2, of which waited for: 3 -> 2; matrix products, arithmetic and copies ran while one was open for 12% -> 4% of each run, Pallas kernels for 0% -> 0%
where the time goes in v1:
time: 186 us
  waiting for transfers between devices  89.1 us (48%)
  blocking collectives  62.3 us (33%)
  matrix products  17.1 us (9%)
  between operations  14 us (8%)
  other arithmetic  2.4 us (1%)
    all_gather x1, waiting for transfers between devices, per_device(): grad_all = lax.all_gather(out_grad, 'row', axis=0, tiled=True)  82 us
    all_to_all x1, blocking collectives, per_device(): lax.all_to_all(jnp.stack([saved_input] * lax.axis_size('col')), 'col', 0, 0)  62.3 us
    dot_general x1, matrix products, per_device(): lax.dot_general(grad_all, weight, (((1,), (1,)), ((), ())), preferred_ele...  9.76 us
    dot_general x1, matrix products, per_device(): lax.dot_general(hidden, grad_all, (((0,), (0,)), ((), ())), preferred_ele...  7.33 us
    reduce_scatter x1, waiting for transfers between devices, per_device(): lax.psum_scatter(lax.dot_general(grad_all, weight, (((1,), (1,)), ((), ()...  6.37 us
  transfers between devices with their start and end apart: 2, of which 2 were waited for; matrix products, arithmetic and copies ran while one was open for 4% of the time, Pallas kernels for 0%

profile of v1, /device:TPU:1, one launch (start us, length us, event | category | flops | bytes accessed | tf_op | source)
XLA Modules:
  0.0 186.3 jit_solution(5535786687496310755)
XLA Ops:
  7.2 0.0 all-gather.2.cloned.1.call-start
  7.2 0.7 all-gather.2.cloned.1.call-update
  7.9 0.0 reduce-scatter.2.cloned.1.call-start
  7.9 82.0 %all-gather.2.cloned.1.call-done = bf16[1024,1536]{1,0:T(8,128)(2,1)} async-done(((bf16[32,1536]{1,0:T(8,128)(2,1)}), bf16[1024,1536]{1,0:T(8,128)(2,1)}) %all-gather.2.cloned.1.call-update) | async-done | bytes 3145744 | tf_op jit(solution)/shard_map/all_gather | solution.py:19
  90.0 9.8 %fusion.23 = f32[1024,1536]{1,0:T(8,128)} fusion(bf16[1024,1536]{1,0:T(8,128)(2,1)} %all-gather.2.cloned.1.call-done, bf16[1536,1536]{1,0:T(8,128)(2,1)} %param.5), kind=kOutput, calls=%fused_computation.35 | convolution fusion | flops 4831838208 | bytes 14155776 | tf_op jit(solution)/shard_map/dot_general | solution.py:29
  99.7 0.0 copy-start
  99.7 0.0 reduce-scatter.2.cloned.1.call-update
  99.7 1.0 copy-done
  100.7 0.0 copy-start.1
  100.7 0.3 stack.2
  101.0 62.3 %all_to_all.5 = bf16[8,128,1536]{2,1,0:T(8,128)(2,1)S(1)} all-to-all(bf16[8,128,1536]{2,1,0:T(8,128)(2,1)S(1)} %stack.2), channel_id=1, replica_groups=mesh['row'=32,'col'=8] {'col'}, dimensions={0} | all-to-all | bytes 6291456 | tf_op jit(solution)/shard_map/all_to_all | solution.py:21
  163.3 0.0 copy-done.1
  163.3 7.3 %convolution_convert_fusion = bf16[1536,1536]{1,0:T(8,128)(2,1)} fusion(bf16[1024,1536]{1,0:T(8,128)(2,1)S(1)} %copy-done.1, bf16[1024,1536]{1,0:T(8,128)(2,1)S(1)} %bitcast.5), kind=kOutput, calls=%fused_computation.5 | convolution fusion | flops 4849926144 | bytes 11010048 | tf_op jit(solution)/shard_map/dot_general | solution.py:25
  170.6 6.4 %reduce-scatter.2.cloned.1.call-done = f32[128,1536]{1,0:T(8,128)} async-done(((f32[1024,1536]{1,0:T(8,128)}), f32[128,1536]{1,0:T(8,128)}) %reduce-scatter.2.cloned.1.call-update) | async-done | bytes 786448 | tf_op jit(solution)/shard_map/reduce_scatter | solution.py:28
  177.0 2.4 %fusion.17 = bf16[128,1536]{1,0:T(8,128)(2,1)} fusion(f32[128,1536]{1,0:T(8,128)} %reduce-scatter.2.cloned.1.call-done, bf16[128,1536]{1,0:T(8,128)(2,1)S(1)} %copy-done), kind=kLoop, calls=%fused_computation.29 | loop fusion | flops 3932160 | bytes 1572864 | tf_op jit(solution)/shard_map/convert_element_type | solution.py:37
Async XLA Ops:
  7.2 82.8 %all-gather.2.cloned.1.call-start = ((), (), s32[]{:S(2)}) async-start(), calls=%async_computation.2 | async-start | bytes 3244032 | tf_op jit(solution)/shard_map/all_gather | solution.py:19
  7.9 169.1 %reduce-scatter.2.cloned.1.call-start = ((), (), s32[]{:S(2)}) async-start(), calls=%async_computation.3 | async-start | bytes 7077888 | tf_op jit(solution)/shard_map/reduce_scatter | solution.py:28
  99.7 1.0 copy-start
  100.7 62.6 %copy-start.1 = (bf16[1024,1536]{1,0:T(8,128)(2,1)S(1)}, bf16[1024,1536]{1,0:T(8,128)(2,1)}, u32[]{:S(2)}) copy-start(bf16[1024,1536]{1,0:T(8,128)(2,1)} %all-gather.2.cloned.1.call-done) | copy-start | bytes 9437188
Sparse Core Ops, SparseCore 0:
  10.5 79.3 all-gather.1
  99.9 77.1 reduce-scatter.1
